TPU v7x, 32 devices: a whole 2x2x4 slice. The times are simulated.
32 devices in a mesh: chan: 4 (over y, x), tm: 8 (over z, core).
Axes of the slice: x: 2, y: 2, z: 4, core: 2. Of those that a mesh axis runs over, the one named last changes fastest.
Arguments:
- raw_samples: float32 [32, 512, 2048], P('tm', 'chan'), may hold values from -80 to 80
Outputs:
- correlations: float32 [512, 512, 256], P(('chan', 'tm'))
All inputs are finite; a program needn't handle non-finite values.
Results may differ from a plain program's by a relative error of at most 0.0043.
Values may be sent and summed in bfloat16 or wider, within the bound.
No kernel may reach another device: no remote copies, remote signals or barrier semaphores. Data moves between devices by JAX's collectives and lax.ppermute only.
A program may use at most 192 MiB of HBM per device.

v0:
```python
import math
import jax
import jax.numpy as jnp
from jax import lax
from jax.sharding import PartitionSpec as P

LAGS = 256


def spread(value, axis, source):
    kept = jnp.where(lax.axis_index(axis) == source, value, 0).astype(value.dtype)
    return lax.psum(kept, axis)


def decimate(raw_samples):
    even_taps = raw_samples[..., 0::2]
    odd_taps = raw_samples[..., 1::2]
    odd_before = jnp.concatenate([jnp.zeros_like(odd_taps[..., :1]), odd_taps[..., :-1]], axis=-1)
    return 0.25 * odd_before + 0.5 * even_taps + 0.25 * odd_taps


def whiten(real_part, imag_part):
    power = real_part * real_part + imag_part * imag_part
    level = jnp.mean(power, axis=-1, keepdims=True)
    factor = 1.0 / jnp.sqrt(power + 0.1 * level + 1e-06)
    return (real_part * factor, imag_part * factor)


def lag_table(freq_count, sample_count, lag_count):
    freq_index = jnp.arange(1, freq_count + 1, dtype=jnp.int32)
    lag_index = jnp.arange(lag_count, dtype=jnp.int32) - lag_count // 2
    turns = freq_index[:, None] * (lag_index[None, :] % sample_count) % sample_count
    angle = turns.astype(jnp.float32) * (2.0 * math.pi / sample_count)
    return jnp.concatenate([jnp.cos(angle), -jnp.sin(angle)], axis=0).astype(jnp.bfloat16)


def transform_tables(sample_count, freq_count):
    time_index = jnp.arange(sample_count, dtype=jnp.int32)
    freq_index = jnp.arange(1, freq_count + 1, dtype=jnp.int32)
    turns = time_index[:, None] * freq_index[None, :] % sample_count
    angle = turns.astype(jnp.float32) * (2.0 * math.pi / sample_count)
    return (jnp.cos(angle), -jnp.sin(angle))


def cross_block(local_spec, turned_spec, remote_spec):
    real_cross = jnp.einsum(
        "sik,sjk->ijk", local_spec, remote_spec, preferred_element_type=jnp.float32
    )
    imag_cross = jnp.einsum(
        "sik,sjk->ijk", turned_spec, remote_spec, preferred_element_type=jnp.float32
    )
    return jnp.concatenate([real_cross, imag_cross], axis=-1).astype(jnp.bfloat16)


def per_device(raw_samples):
    seg_count, block_width, raw_length = raw_samples.shape
    sample_count = raw_length // 2
    freq_count = sample_count // 8
    chan_count = lax.axis_size("chan")
    time_count = lax.axis_size("tm")
    channel_total = block_width * chan_count
    signal = decimate(raw_samples).reshape(seg_count * block_width, sample_count)
    cos_table, sin_table = transform_tables(sample_count, freq_count)
    real_part = jnp.dot(
        signal, cos_table, precision=lax.Precision.HIGHEST, preferred_element_type=jnp.float32
    )
    imag_part = jnp.dot(
        signal, sin_table, precision=lax.Precision.HIGHEST, preferred_element_type=jnp.float32
    )
    real_part = real_part.reshape(seg_count, block_width, freq_count)
    imag_part = imag_part.reshape(seg_count, block_width, freq_count)
    real_w, imag_w = whiten(real_part, imag_part)
    local_spec = jnp.concatenate([real_w, imag_w], axis=0).astype(jnp.bfloat16)
    table = lag_table(freq_count, sample_count, LAGS)
    norm_scale = 1.0 / math.sqrt(freq_count * seg_count * time_count)
    tm_index = lax.axis_index("tm")
    pair_spec = local_spec.reshape(2, seg_count, block_width, freq_count)
    all_spec = lax.all_gather(pair_spec, "tm", axis=1, tiled=True)
    span_width = channel_total // time_count
    span_offset = tm_index * span_width % block_width
    own_span = lax.dynamic_slice_in_dim(all_spec, span_offset, span_width, 2)
    root_block = tm_index * span_width // block_width
    column_spec = spread(own_span, "chan", root_block)

    def add_group(group_index, total):
        seg_start = (group_index * seg_count).astype(jnp.int32)
        left_group = lax.dynamic_slice_in_dim(all_spec, seg_start, seg_count, 1)
        right_group = lax.dynamic_slice_in_dim(column_spec, seg_start, seg_count, 1)
        left_rows = left_group.reshape(2 * seg_count, block_width, freq_count)
        turned_rows = jnp.concatenate([left_group[1], -left_group[0]], axis=0)
        right_rows = right_group.reshape(2 * seg_count, span_width, freq_count)
        return total + cross_block(left_rows, turned_rows, right_rows).astype(jnp.float32)

    summed = lax.fori_loop(
        0, time_count, add_group, jnp.zeros((block_width, span_width, 2 * freq_count), jnp.float32)
    )
    pair_lags = (
        jnp.einsum(
            "ijk,kl->ijl", summed, table.astype(jnp.float32), precision=lax.Precision.HIGHEST
        )
        * norm_scale
    )
    return lax.all_to_all(pair_lags, "tm", split_axis=0, concat_axis=1, tiled=True)


def solution(mesh):
    return jax.shard_map(
        per_device,
        mesh=mesh,
        in_specs=(P("tm", "chan", None),),
        out_specs=P(("chan", "tm"), None, None),
        check_vma=False,
    )
```

profile of v0, /device:TPU:0, one launch (start us, length us, event | category | flops | bytes accessed | tf_op | source)
XLA Modules:
  0.0 571.0 jit_solution(17318905619053049182)
XLA Ops:
  6.5 70.9 %slice.23 = f32[4,128,1024]{2,1,0:T(8,128)S(1)} slice(f32[4,128,2048]{2,1,0:T(8,128)} %param.3), slice={[0:4:1], [0:128:1], [1:2048:2]} | slice | bytes 4194304 | tf_op jit(solution)/shard_map/slice | solution.py:17
  77.4 71.3 %slice.25 = f32[4,128,1024]{2,1,0:T(8,128)} slice(f32[4,128,2048]{2,1,0:T(8,128)} %param.3), slice={[0:4:1], [0:128:1], [0:2048:2]} | slice | bytes 4194304 | tf_op jit(solution)/shard_map/slice | solution.py:16
  148.7 6.3 %fusion.13 = f32[4,128,128]{1,2,0:T(8,128)S(1)} fusion(s32[128]{0:T(128)S(1)} %iota_add_fusion, f32[4,128,1024]{2,1,0:T(8,128)S(1)} %slice.23, f32[4,128,1024]{2,1,0:T(8,128)} %slice.25, f32[4,128,1023]{2,1,0:T(8,128)S(1)} %bitcast.48), kind=kOutput, calls=%fused_computation.24 | convolution fusion | flops 809762816 | bytes 6552064 | tf_op jit(solution)/shard_map/dot_general | solution.py:64
  155.1 4.7 fusion.23
  160.9 31.9 %all-gather.2.cloned.1.call-done = bf16[2,32,128,128]{3,2,0,1:T(8,128)(2,1)} async-done(((bf16[2,4,128,128]{3,2,0,1:T(8,128)(2,1)}), bf16[2,32,128,128]{3,2,0,1:T(8,128)(2,1)}) %all-gather.2.cloned.1.call-update) | async-done | bytes 2097168 | tf_op jit(solution)/shard_map/all_gather | solution.py:78
  192.7 2.6 dynamic-slice_select_fusion
  196.0 51.9 %all-reduce.3.cloned.1.call-done = bf16[2,32,64,128]{3,2,0,1:T(8,128)(2,1)} async-done(((bf16[2,32,64,128]{3,2,0,1:T(8,128)(2,1)}), bf16[2,32,64,128]{3,2,0,1:T(8,128)(2,1)}) %all-reduce.3.cloned.1.call-update) | async-done | bytes 1048592 | tf_op jit(solution)/shard_map/psum | solution.py:12
  247.9 104.6 %while.14 = (s32[]{:T(128)}, f32[128,64,256]{0,1,2:T(8,128)}, bf16[2,32,64,128]{3,2,0,1:T(8,128)(2,1)}, bf16[2,32,128,128]{3,2,0,1:T(8,128)(2,1)}, s32[]{:T(128)}, /*index=5*/s32[]{:T(128)}, s32[]{:T(128)}, s32[]{:T(128)}, s32[]{}) while((s32[]{:T(128)}, f32[128,64,256]{0,1,2:T(8,128)}, bf16[2,32,64,128]{3,2,0,1:T(8,128)(2,1)}, ...), condition=%wide.region_3.4_spmd.clone, body=%wide.region_2.3_spmd.clone.sunk | while | flops 44630024 | bytes 28573872 | solution.py:94
  252.2 2.1 convert_bitcast_fusion.5
  254.3 5.3 select_add_fusion.2
  264.0 2.1 convert_bitcast_fusion.5
  266.0 6.8 %select_add_fusion.2 = f32[128,64,256]{0,1,2:T(8,128)} fusion(f32[128,64,256]{0,1,2:T(8,128)} %get-tuple-element.163, bf16[128,64,128]{0,1,2:T(8,128)(2,1)S(1)} %convert_bitcast_fusion.4, bf16[128,64,128]{0,1,2:T(8,128)(2,1)} %convert_bitcast_fusion.5, pred[]{:T(512)S(6)} %compare.13), kind=kLoop, calls=%fused_computation.clone.1 | loop fusion | flops 8388608 | bytes 20971520 | tf_op jit(solution)/shard_map/while/body/eval_jaxpr/add | solution.py:92
  277.2 2.1 convert_bitcast_fusion.5
  279.3 6.8 %select_add_fusion.2 = f32[128,64,256]{0,1,2:T(8,128)} fusion(f32[128,64,256]{0,1,2:T(8,128)} %get-tuple-element.163, bf16[128,64,128]{0,1,2:T(8,128)(2,1)S(1)} %convert_bitcast_fusion.4, bf16[128,64,128]{0,1,2:T(8,128)(2,1)} %convert_bitcast_fusion.5, pred[]{:T(512)S(6)} %compare.13), kind=kLoop, calls=%fused_computation.clone.1 | loop fusion | flops 8388608 | bytes 20971520 | tf_op jit(solution)/shard_map/while/body/eval_jaxpr/add | solution.py:92
  292.6 6.8 %select_add_fusion.2 = f32[128,64,256]{0,1,2:T(8,128)} fusion(f32[128,64,256]{0,1,2:T(8,128)} %get-tuple-element.163, bf16[128,64,128]{0,1,2:T(8,128)(2,1)S(1)} %convert_bitcast_fusion.4, bf16[128,64,128]{0,1,2:T(8,128)(2,1)} %convert_bitcast_fusion.5, pred[]{:T(512)S(6)} %compare.13), kind=kLoop, calls=%fused_computation.clone.1 | loop fusion | flops 8388608 | bytes 20971520 | tf_op jit(solution)/shard_map/while/body/eval_jaxpr/add | solution.py:92
  305.8 6.8 %select_add_fusion.2 = f32[128,64,256]{0,1,2:T(8,128)} fusion(f32[128,64,256]{0,1,2:T(8,128)} %get-tuple-element.163, bf16[128,64,128]{0,1,2:T(8,128)(2,1)S(1)} %convert_bitcast_fusion.4, bf16[128,64,128]{0,1,2:T(8,128)(2,1)} %convert_bitcast_fusion.5, pred[]{:T(512)S(6)} %compare.13), kind=kLoop, calls=%fused_computation.clone.1 | loop fusion | flops 8388608 | bytes 20971520 | tf_op jit(solution)/shard_map/while/body/eval_jaxpr/add | solution.py:92
  319.1 6.8 %select_add_fusion.2 = f32[128,64,256]{0,1,2:T(8,128)} fusion(f32[128,64,256]{0,1,2:T(8,128)} %get-tuple-element.163, bf16[128,64,128]{0,1,2:T(8,128)(2,1)S(1)} %convert_bitcast_fusion.4, bf16[128,64,128]{0,1,2:T(8,128)(2,1)} %convert_bitcast_fusion.5, pred[]{:T(512)S(6)} %compare.13), kind=kLoop, calls=%fused_computation.clone.1 | loop fusion | flops 8388608 | bytes 20971520 | tf_op jit(solution)/shard_map/while/body/eval_jaxpr/add | solution.py:92
  332.4 6.8 %select_add_fusion.2 = f32[128,64,256]{0,1,2:T(8,128)} fusion(f32[128,64,256]{0,1,2:T(8,128)} %get-tuple-element.163, bf16[128,64,128]{0,1,2:T(8,128)(2,1)S(1)} %convert_bitcast_fusion.4, bf16[128,64,128]{0,1,2:T(8,128)(2,1)} %convert_bitcast_fusion.5, pred[]{:T(512)S(6)} %compare.13), kind=kLoop, calls=%fused_computation.clone.1 | loop fusion | flops 8388608 | bytes 20971520 | tf_op jit(solution)/shard_map/while/body/eval_jaxpr/add | solution.py:92
  343.6 2.1 convert_bitcast_fusion.5
  345.6 6.8 %select_add_fusion.2 = f32[128,64,256]{0,1,2:T(8,128)} fusion(f32[128,64,256]{0,1,2:T(8,128)} %get-tuple-element.163, bf16[128,64,128]{0,1,2:T(8,128)(2,1)S(1)} %convert_bitcast_fusion.4, bf16[128,64,128]{0,1,2:T(8,128)(2,1)} %convert_bitcast_fusion.5, pred[]{:T(512)S(6)} %compare.13), kind=kLoop, calls=%fused_computation.clone.1 | loop fusion | flops 8388608 | bytes 20971520 | tf_op jit(solution)/shard_map/while/body/eval_jaxpr/add | solution.py:92
  352.5 14.2 %broadcast_multiply_fusion = f32[128,64,256]{2,0,1:T(8,128)S(1)} fusion(f32[128,64,256]{0,1,2:T(8,128)} %get-tuple-element.84, bf16[128,256]{1,0:T(8,128)(2,1)S(1)} %get-tuple-element.121, bf16[128,256]{1,0:T(8,128)(2,1)S(1)} %get-tuple-element.120), kind=kOutput, calls=%fused_computation.13 | convolution fusion | flops 6444810240 | bytes 16908288 | tf_op jit(solution)/shard_map/ijk,kl->ijl/dot_general | solution.py:98
  366.7 4.9 copy.12
  371.6 188.5 %all_to_all.18 = f32[128,64,256]{2,1,0:T(8,128)S(1)} all-to-all(f32[128,64,256]{2,1,0:T(8,128)S(1)} %copy.12), channel_id=1, replica_groups=mesh['chan'=4,'tm'=8] {'tm'}, dimensions={0} | all-to-all | bytes 16777216 | tf_op jit(solution)/shard_map/all_to_all | solution.py:103
  560.1 4.0 copy.13
  (82 shorter events, 44.5 us)
Async XLA Ops:
  6.5 186.2 %all-gather.2.cloned.1.call-start = ((), (), s32[]{:S(2)}) async-start(), calls=%async_computation.1 | async-start | bytes 2359296 | tf_op jit(solution)/shard_map/all_gather | solution.py:78
  148.7 6.3 %copy-start = (f32[4,128,1024]{2,1,0:T(8,128)S(1)}, f32[4,128,1024]{2,1,0:T(8,128)}, u32[]{:S(2)}) copy-start(f32[4,128,1024]{2,1,0:T(8,128)} %slice.25) | copy-start | bytes 6291460
  160.8 87.1 %all-reduce.3.cloned.1.call-start = ((), (), s32[]{:S(2)}) async-start(), calls=%async_computation.2 | async-start | bytes 2097152 | tf_op jit(solution)/shard_map/psum | solution.py:12
Sparse Core Ops, SparseCore 0:
  160.9 31.7 all-gather.1
  195.8 52.0 all-reduce.2
where the time goes:
time: 572 us; the launch traced here: 571 us
  blocking collectives  189 us (33%)
  local copies, waits for them, and re-layouts  172 us (30%)
  waiting for transfers between devices  83.8 us (15%)
  other arithmetic  64.5 us (11%)
  matrix products  47.8 us (8%)
  between operations  13.5 us (2%)
    all_to_all x1, blocking collectives, per_device(): lax.all_to_all(pair_lags, 'tm', split_axis=0, concat_axis=1, tiled=True)  189 us
    slice x1, local copies, waits for them, and re-layouts, decimate(): even_taps = raw_samples[..., 0::2]  71.3 us
    slice x1, local copies, waits for them, and re-layouts, decimate(): odd_taps = raw_samples[..., 1::2]  70.9 us
    add x8, other arithmetic, add_group(): total + cross_block(left_rows, turned_rows, right_rows).astype(jnp.float32)  53.2 us
    psum x1, waiting for transfers between devices, spread(): return lax.psum(kept, axis)  51.9 us
    all_gather x1, waiting for transfers between devices, per_device(): all_spec = lax.all_gather(pair_spec, 'tm', axis=1, tiled=True)  31.9 us
    dot_general x8, matrix products, cross_block(): jnp.einsum('sik,sjk->ijk', local_spec, remote_spec, preferred_element_typ...  16.6 us
    dot_general x1, matrix products, per_device(): jnp.einsum('ijk,kl->ijl', summed, table.astype(jnp.float32), precision=la...  14.2 us
  transfers between devices with their start and end apart: 2, of which 2 were waited for; matrix products, arithmetic and copies ran while one was open for 0% of the time, Pallas kernels for 0%

commit v1 on v0

--- a/solution.py
+++ b/solution.py
@@ -75,7 +75,21 @@
     norm_scale = 1.0 / math.sqrt(freq_count * seg_count * time_count)
     tm_index = lax.axis_index("tm")
     pair_spec = local_spec.reshape(2, seg_count, block_width, freq_count)
-    all_spec = lax.all_gather(pair_spec, "tm", axis=1, tiled=True)
+    ways, here, hop = (lax.axis_size("tm"), lax.axis_index("tm"), pair_spec.shape[1])
+    shape = [n * ways if d == 1 else n for d, n in enumerate(pair_spec.shape)]
+    full = lax.dynamic_update_slice_in_dim(
+        jnp.zeros(shape, pair_spec.dtype), pair_spec, here * hop, axis=1
+    )
+    going_up = going_down = pair_spec
+    for far in range(1, ways // 2 + 1):
+        going_up = lax.ppermute(going_up, "tm", [(d, (d + 1) % ways) for d in range(ways)])
+        full = lax.dynamic_update_slice_in_dim(full, going_up, (here - far) % ways * hop, axis=1)
+        if 2 * far < ways:
+            going_down = lax.ppermute(going_down, "tm", [(d, (d - 1) % ways) for d in range(ways)])
+            full = lax.dynamic_update_slice_in_dim(
+                full, going_down, (here + far) % ways * hop, axis=1
+            )
+    all_spec = full
     span_width = channel_total // time_count
     span_offset = tm_index * span_width % block_width
     own_span = lax.dynamic_slice_in_dim(all_spec, span_offset, span_width, 2)

time: 572 us -> 592 us (1.035)
  starting transfers between devices: 0.04 us -> 12.1 us
  local copies, waits for them, and re-layouts: 172 us -> 180 us
    all_gather x1 -> x0, waiting for transfers between devices: 31.9 us -> none  [per_device(): all_spec = lax.all_gather(pair_spec, 'tm', axis=1, tiled=True)]
    psum x1, waiting for transfers between devices: 51.9 us -> 69.2 us  [spread(): return lax.psum(kept, axis)]
    ppermute x0 -> x7, waiting for transfers between devices: none -> 13.3 us  [the longest x4 10.2 us: per_device(): lax.ppermute(going_up, 'tm', [(d, (d + 1) % ways) for d in range(ways)])]
    ppermute x0 -> x7, starting transfers between devices: none -> 12.1 us  [the longest x3 11.6 us: per_device(): lax.ppermute(going_down, 'tm', [(d, (d - 1) % ways) for d in range(ways)])]
    squeeze x0 -> x8, other arithmetic: none -> 9.54 us  [add_group(): turned_rows = jnp.concatenate([left_group[1], -left_group[0]], axis=0)]
    slice x8 -> x0, other arithmetic: 7.96 us -> none  [add_group(): turned_rows = jnp.concatenate([left_group[1], -left_group[0]], axis=0)]
    dynamic_update_slice x0 -> x8, local copies, waits for them, and re-layouts: none -> 6.65 us  [the longest x4 3.35 us: per_device(): lax.dynamic_update_slice_in_dim(full, going_up, (here - far) % ways * hop...]
  transfers between devices with their start and end apart: 2 -> 8, of which waited for: 2 -> 7; matrix products, arithmetic and copies ran while one was open for 0% -> 1% of each run, Pallas kernels for 0% -> 0%
where the time goes in v1:
time: 592 us; the launch traced here: 591 us
  blocking collectives  189 us (32%)
  local copies, waits for them, and re-layouts  180 us (30%)
  waiting for transfers between devices  82.5 us (14%)
  other arithmetic  67.3 us (11%)
  matrix products  46.8 us (8%)
  between operations  13.5 us (2%)
  starting transfers between devices  12.1 us (2%)
    all_to_all x1, blocking collectives, per_device(): lax.all_to_all(pair_lags, 'tm', split_axis=0, concat_axis=1, tiled=True)  189 us
    slice x1, local copies, waits for them, and re-layouts, decimate(): even_taps = raw_samples[..., 0::2]  71.3 us
    slice x1, local copies, waits for them, and re-layouts, decimate(): odd_taps = raw_samples[..., 1::2]  70.9 us
    psum x1, waiting for transfers between devices, spread(): return lax.psum(kept, axis)  69.2 us
    add x8, other arithmetic, add_group(): total + cross_block(left_rows, turned_rows, right_rows).astype(jnp.float32)  53.2 us
    dot_general x8, matrix products, cross_block(): jnp.einsum('sik,sjk->ijk', local_spec, remote_spec, preferred_element_typ...  16.6 us
    dot_general x1, matrix products, per_device(): jnp.einsum('ijk,kl->ijl', summed, table.astype(jnp.float32), precision=la...  14.2 us
  transfers between devices with their start and end apart: 8, of which 7 were waited for; matrix products, arithmetic and copies ran while one was open for 1% of the time, Pallas kernels for 0%

profile of v1, /device:TPU:0, one launch (start us, length us, event | category | flops | bytes accessed | tf_op | source)
XLA Modules:
  0.0 590.9 jit_solution(5452748174097003109)
XLA Ops:
  6.5 70.9 %slice.23 = f32[4,128,1024]{2,1,0:T(8,128)S(1)} slice(f32[4,128,2048]{2,1,0:T(8,128)} %param.3), slice={[0:4:1], [0:128:1], [1:2048:2]} | slice | bytes 4194304 | tf_op jit(solution)/shard_map/slice | solution.py:17
  77.4 71.3 %slice.25 = f32[4,128,1024]{2,1,0:T(8,128)} slice(f32[4,128,2048]{2,1,0:T(8,128)} %param.3), slice={[0:4:1], [0:128:1], [0:2048:2]} | slice | bytes 4194304 | tf_op jit(solution)/shard_map/slice | solution.py:16
  148.7 5.7 fusion.14
  154.5 4.1 fusion.24
  159.5 4.1 collective-permute-start.1
  163.6 4.2 collective-permute-done
  168.3 3.8 collective-permute-start.3
  177.2 3.7 collective-permute-start.5
  188.3 3.6 collective-permute-done.6
  192.7 3.7 dynamic-slice_select_fusion
  197.0 69.2 %all-reduce.3.cloned.1.call-done = bf16[2,32,64,128]{2,1,3,0:T(8,128)(2,1)} async-done(((bf16[2,32,64,128]{2,1,3,0:T(8,128)(2,1)}), bf16[2,32,64,128]{2,1,3,0:T(8,128)(2,1)}) %all-reduce.3.cloned.1.call-update) | async-done | bytes 1048592 | tf_op jit(solution)/shard_map/psum | solution.py:12
  266.2 106.2 %while.14 = (s32[]{:T(128)}, f32[128,64,256]{0,1,2:T(8,128)}, bf16[2,32,64,128]{2,1,3,0:T(8,128)(2,1)}, bf16[2,32,128,128]{2,1,3,0:T(8,128)(2,1)}, s32[]{:T(128)}, /*index=5*/s32[]{:T(128)}, s32[]{:T(128)}, s32[]{:T(128)}, s32[]{}) while((s32[]{:T(128)}, f32[128,64,256]{0,1,2:T(8,128)}, bf16[2,32,64,128]{2,1,3,0:T(8,128)(2,1)}, ...), condition=%wide.region_3.4_spmd.clone, body=%wide.region_2.3_spmd.clone.sunk | while | flops 44761096 | bytes 28049584 | solution.py:108
  272.9 5.3 select_add_fusion.2
  284.8 6.8 %select_add_fusion.2 = f32[128,64,256]{0,1,2:T(8,128)} fusion(f32[128,64,256]{0,1,2:T(8,128)} %get-tuple-element.163, bf16[128,64,128]{0,1,2:T(8,128)(2,1)S(1)} %convert_bitcast_fusion.4, bf16[128,64,128]{0,1,2:T(8,128)(2,1)} %convert_bitcast_fusion.5, pred[]{:T(512)S(6)} %compare.20), kind=kLoop, calls=%fused_computation.clone.1 | loop fusion | flops 8388608 | bytes 20971520 | tf_op jit(solution)/shard_map/while/body/eval_jaxpr/add | solution.py:106
  298.2 6.8 %select_add_fusion.2 = f32[128,64,256]{0,1,2:T(8,128)} fusion(f32[128,64,256]{0,1,2:T(8,128)} %get-tuple-element.163, bf16[128,64,128]{0,1,2:T(8,128)(2,1)S(1)} %convert_bitcast_fusion.4, bf16[128,64,128]{0,1,2:T(8,128)(2,1)} %convert_bitcast_fusion.5, pred[]{:T(512)S(6)} %compare.20), kind=kLoop, calls=%fused_computation.clone.1 | loop fusion | flops 8388608 | bytes 20971520 | tf_op jit(solution)/shard_map/while/body/eval_jaxpr/add | solution.py:106
  311.7 6.8 %select_add_fusion.2 = f32[128,64,256]{0,1,2:T(8,128)} fusion(f32[128,64,256]{0,1,2:T(8,128)} %get-tuple-element.163, bf16[128,64,128]{0,1,2:T(8,128)(2,1)S(1)} %convert_bitcast_fusion.4, bf16[128,64,128]{0,1,2:T(8,128)(2,1)} %convert_bitcast_fusion.5, pred[]{:T(512)S(6)} %compare.20), kind=kLoop, calls=%fused_computation.clone.1 | loop fusion | flops 8388608 | bytes 20971520 | tf_op jit(solution)/shard_map/while/body/eval_jaxpr/add | solution.py:106
  325.2 6.8 %select_add_fusion.2 = f32[128,64,256]{0,1,2:T(8,128)} fusion(f32[128,64,256]{0,1,2:T(8,128)} %get-tuple-element.163, bf16[128,64,128]{0,1,2:T(8,128)(2,1)S(1)} %convert_bitcast_fusion.4, bf16[128,64,128]{0,1,2:T(8,128)(2,1)} %convert_bitcast_fusion.5, pred[]{:T(512)S(6)} %compare.20), kind=kLoop, calls=%fused_computation.clone.1 | loop fusion | flops 8388608 | bytes 20971520 | tf_op jit(solution)/shard_map/while/body/eval_jaxpr/add | solution.py:106
  338.6 6.8 %select_add_fusion.2 = f32[128,64,256]{0,1,2:T(8,128)} fusion(f32[128,64,256]{0,1,2:T(8,128)} %get-tuple-element.163, bf16[128,64,128]{0,1,2:T(8,128)(2,1)S(1)} %convert_bitcast_fusion.4, bf16[128,64,128]{0,1,2:T(8,128)(2,1)} %convert_bitcast_fusion.5, pred[]{:T(512)S(6)} %compare.20), kind=kLoop, calls=%fused_computation.clone.1 | loop fusion | flops 8388608 | bytes 20971520 | tf_op jit(solution)/shard_map/while/body/eval_jaxpr/add | solution.py:106
  352.1 6.8 %select_add_fusion.2 = f32[128,64,256]{0,1,2:T(8,128)} fusion(f32[128,64,256]{0,1,2:T(8,128)} %get-tuple-element.163, bf16[128,64,128]{0,1,2:T(8,128)(2,1)S(1)} %convert_bitcast_fusion.4, bf16[128,64,128]{0,1,2:T(8,128)(2,1)} %convert_bitcast_fusion.5, pred[]{:T(512)S(6)} %compare.20), kind=kLoop, calls=%fused_computation.clone.1 | loop fusion | flops 8388608 | bytes 20971520 | tf_op jit(solution)/shard_map/while/body/eval_jaxpr/add | solution.py:106
  365.6 6.8 %select_add_fusion.2 = f32[128,64,256]{0,1,2:T(8,128)} fusion(f32[128,64,256]{0,1,2:T(8,128)} %get-tuple-element.163, bf16[128,64,128]{0,1,2:T(8,128)(2,1)S(1)} %convert_bitcast_fusion.4, bf16[128,64,128]{0,1,2:T(8,128)(2,1)} %convert_bitcast_fusion.5, pred[]{:T(512)S(6)} %compare.20), kind=kLoop, calls=%fused_computation.clone.1 | loop fusion | flops 8388608 | bytes 20971520 | tf_op jit(solution)/shard_map/while/body/eval_jaxpr/add | solution.py:106
  372.4 14.2 %broadcast_multiply_fusion = f32[128,64,256]{2,0,1:T(8,128)S(1)} fusion(f32[128,64,256]{0,1,2:T(8,128)} %get-tuple-element.84, bf16[128,256]{1,0:T(8,128)(2,1)S(1)} %get-tuple-element.121, bf16[128,256]{1,0:T(8,128)(2,1)S(1)} %get-tuple-element.120), kind=kOutput, calls=%fused_computation.14 | convolution fusion | flops 6444810240 | bytes 16908288 | tf_op jit(solution)/shard_map/ijk,kl->ijl/dot_general | solution.py:112
  386.6 4.9 copy.15
  391.5 188.5 %all_to_all.18 = f32[128,64,256]{2,1,0:T(8,128)S(1)} all-to-all(f32[128,64,256]{2,1,0:T(8,128)S(1)} %copy.15), channel_id=1, replica_groups=mesh['chan'=4,'tm'=8] {'tm'}, dimensions={0} | all-to-all | bytes 16777216 | tf_op jit(solution)/shard_map/all_to_all | solution.py:117
  580.0 4.0 copy.16
  (86 shorter events, 68.0 us)
Async XLA Ops:
  6.5 259.7 %all-reduce.3.cloned.1.call-start = ((), (), s32[]{:S(2)}) async-start(), calls=%async_computation.1 | async-start | bytes 4194304 | tf_op jit(solution)/shard_map/psum | solution.py:12
  148.7 5.8 copy-start
  159.0 8.8 %collective-permute-start = (bf16[2,4,128,128]{2,1,3,0:T(4,128)(2,1)S(1)}, bf16[2,4,128,128]{2,1,3,0:T(4,128)(2,1)S(1)}, u32[]{:S(2)}, u32[]{:S(2)}) collective-permute-start(bf16[2,4,128,128]{2,1,3,0:T(4,128)(2,1)S(1)} %copy.10), channel_id=1, source_target_pairs={{0,1},{1,2},{2,3},{3,4},{4,5},{5,6},{6,7},{7,0},{8,9},{9,10},{10,1... | collective-permute-start | bytes 786440 | tf_op jit(solution)/shard_map/ppermute | solution.py:85
  159.5 8.7 %collective-permute-start.1 = (bf16[2,4,128,128]{2,1,3,0:T(4,128)(2,1)S(1)}, bf16[2,4,128,128]{2,1,3,0:T(4,128)(2,1)S(1)}, u32[]{:S(2)}, u32[]{:S(2)}) collective-permute-start(bf16[2,4,128,128]{2,1,3,0:T(4,128)(2,1)S(1)} %copy.10), channel_id=1, source_target_pairs={{0,7},{1,0},{2,1},{3,2},{4,3},{5,4},{6,5},{7,6},{8,15},{9,8},{10,9... | collective-permute-start | bytes 786440 | tf_op jit(solution)/shard_map/ppermute | solution.py:88
  167.8 7.7 %collective-permute-start.2 = (bf16[2,4,128,128]{2,1,3,0:T(4,128)(2,1)S(1)}, bf16[2,4,128,128]{2,1,3,0:T(4,128)(2,1)S(1)}, u32[]{:S(2)}, u32[]{:S(2)}) collective-permute-start(bf16[2,4,128,128]{2,1,3,0:T(4,128)(2,1)S(1)} %collective-permute-done), channel_id=1, source_target_pairs={{0,1},{1,2},{2,3},{3,4},{4,5},{5,6},{6,7},{7,0},{8,9},{9,10},{10,1... | collective-permute-start | bytes 786440 | tf_op jit(solution)/shard_map/ppermute | solution.py:85
  168.3 8.9 %collective-permute-start.3 = (bf16[2,4,128,128]{2,1,3,0:T(4,128)(2,1)S(1)}, bf16[2,4,128,128]{2,1,3,0:T(4,128)(2,1)S(1)}, u32[]{:S(2)}, u32[]{:S(2)}) collective-permute-start(bf16[2,4,128,128]{2,1,3,0:T(4,128)(2,1)S(1)} %collective-permute-done.1), channel_id=1, source_target_pairs={{0,7},{1,0},{2,1},{3,2},{4,3},{5,4},{6,5},{7,6},{8,15},{9,8},{10,9... | collective-permute-start | bytes 786440 | tf_op jit(solution)/shard_map/ppermute | solution.py:88
  175.5 7.7 %collective-permute-start.4 = (bf16[2,4,128,128]{2,1,3,0:T(4,128)(2,1)S(1)}, bf16[2,4,128,128]{2,1,3,0:T(4,128)(2,1)S(1)}, u32[]{:S(2)}, u32[]{:S(2)}) collective-permute-start(bf16[2,4,128,128]{2,1,3,0:T(4,128)(2,1)S(1)} %collective-permute-done.2), channel_id=1, source_target_pairs={{0,1},{1,2},{2,3},{3,4},{4,5},{5,6},{6,7},{7,0},{8,9},{9,10},{10,1... | collective-permute-start | bytes 786440 | tf_op jit(solution)/shard_map/ppermute | solution.py:85
  177.2 10.3 %collective-permute-start.5 = (bf16[2,4,128,128]{2,1,3,0:T(4,128)(2,1)S(1)}, bf16[2,4,128,128]{2,1,3,0:T(4,128)(2,1)S(1)}, u32[]{:S(2)}, u32[]{:S(2)}) collective-permute-start(bf16[2,4,128,128]{2,1,3,0:T(4,128)(2,1)S(1)} %collective-permute-done.3), channel_id=1, source_target_pairs={{0,7},{1,0},{2,1},{3,2},{4,3},{5,4},{6,5},{7,6},{8,15},{9,8},{10,9... | collective-permute-start | bytes 786440 | tf_op jit(solution)/shard_map/ppermute | solution.py:88
  183.2 8.6 %collective-permute-start.6 = (bf16[2,4,128,128]{2,1,3,0:T(4,128)(2,1)S(1)}, bf16[2,4,128,128]{2,1,3,0:T(4,128)(2,1)S(1)}, u32[]{:S(2)}, u32[]{:S(2)}) collective-permute-start(bf16[2,4,128,128]{2,1,3,0:T(4,128)(2,1)S(1)} %collective-permute-done.4), channel_id=1, source_target_pairs={{0,1},{1,2},{2,3},{3,4},{4,5},{5,6},{6,7},{7,0},{8,9},{9,10},{10,1... | collective-permute-start | bytes 786440 | tf_op jit(solution)/shard_map/ppermute | solution.py:85
Sparse Core Ops, SparseCore 0:
  196.5 69.6 all-reduce.2
